TPU v7x, 128 devices: a whole 4x4x4 slice. The times are simulated.
128 devices in a mesh: space: 64 (over y, z_hi, x, core), vec: 2 (over z_lo).
Axes of the slice: x: 4, y: 4, z: 4 (z_hi: 2, z_lo: 2; z = z_hi * 2 + z_lo), core: 2. Of those that a mesh axis runs over, the one named last changes fastest.
Arguments:
- potential: float32 [64, 128, 256], P('space'), may hold values from -8.25 to 8.25
- start_basis: float32 [16, 64, 128, 256], P('vec', 'space'), may hold values from -6 to 6
Outputs:
- new_basis: float32 [16, 64, 128, 256], P('vec', 'space')
- rayleigh: float32 [16, 16], replicated
All inputs are finite; a program needn't handle non-finite values.
Results may differ from a plain program's by a relative error of at most 0.0003.
Values sent between devices are 32-bit elements; how exact they have to be, the bound alone decides.
No kernel may reach another device: no remote copies, remote signals or barrier semaphores. Data moves between devices by JAX's collectives and lax.ppermute only.
A program may use at most 64 MiB of HBM per device.

v0:
```python
import jax
import jax.numpy as jnp
from jax import lax
from jax.sharding import PartitionSpec as P

NSWEEP = 3
SIGMA = 0.5
PREC = lax.Precision.HIGHEST


def extended(value, sides, width):
    for axis, dim in sides:
        peers, length = (lax.axis_size(axis), value.shape[dim])
        up = [(i, (i + 1) % peers) for i in range(peers)]
        down = [(j, i) for i, j in up]
        last = lax.slice_in_dim(value, length - width, length, axis=dim)
        first = lax.slice_in_dim(value, 0, width, axis=dim)
        before = lax.ppermute(last, axis, up)
        after = lax.ppermute(first, axis, down)
        value = jnp.concatenate([before, value, after], axis=dim)
    return value


def local_inner(left, right, scale):
    return jnp.einsum("kzyx,jzyx->kj", left, right, precision=PREC) * scale


def combine(coeff, vectors):
    return jnp.einsum("kj,kzyx->jzyx", coeff, vectors, precision=PREC)


def stencil(padded, potential):
    center = padded[:, 1:-1]
    beside = padded[:, 2:] + padded[:, :-2]
    beside = beside + jnp.roll(center, 1, 2) + jnp.roll(center, -1, 2)
    beside = beside + jnp.roll(center, 1, 3) + jnp.roll(center, -1, 3)
    return potential * center - beside


def inverse_factor(gram):
    lower = jnp.linalg.cholesky(gram)
    return jax.scipy.linalg.solve_triangular(
        lower, jnp.eye(gram.shape[0], dtype=jnp.float32), lower=True
    )


def local(potential, start_basis):
    mine = start_basis.shape[0]
    scale = 1.0 / (
        start_basis.shape[1] * start_basis.shape[2] * start_basis.shape[3] * lax.axis_size("space")
    )
    first = lax.axis_index("vec") * mine
    whole = lax.all_gather(start_basis, "vec", axis=0, tiled=True)
    gram = lax.psum(local_inner(whole, whole, scale), "space")
    basis_all = combine(inverse_factor(gram).T, whole)
    basis = lax.dynamic_slice_in_dim(basis_all, first, mine, 0)
    shifted = jnp.where(potential >= SIGMA, potential - SIGMA + 6.0, potential - SIGMA - 6.0)
    padded = extended(basis, (("space", 1),), 1)
    image = stencil(padded, potential)
    panel = lax.psum(local_inner(basis_all, image, scale), "space")
    rayleigh = lax.all_gather(panel, "vec", axis=1, tiled=True)
    panel_mine = lax.dynamic_slice_in_dim(rayleigh, first, mine, 1)
    resid = image - combine(panel_mine, basis_all)
    correction = jnp.zeros_like(basis)
    for sweep in range(NSWEEP):
        coeff = lax.psum(local_inner(basis_all, correction, scale), "space")
        proj = correction - combine(coeff, basis_all)
        padded = extended(proj, (("space", 1),), 1)
        moved = stencil(padded, potential) - SIGMA * proj
        back = lax.psum(local_inner(basis_all, moved, scale), "space")
        update = -resid - (moved - combine(back, basis_all))
        correction = correction + update / shifted
    proj_two = lax.psum(local_inner(basis_all, correction, scale), "space")
    fresh = correction - combine(proj_two, basis_all)
    fresh_all = lax.all_gather(fresh, "vec", axis=0, tiled=True)
    gram_two = lax.psum(local_inner(fresh_all, fresh_all, scale), "space")
    inverse_two = inverse_factor(gram_two)
    rows_mine = lax.dynamic_slice_in_dim(inverse_two, first, mine, 0)
    new_basis = combine(rows_mine.T, fresh_all)
    return (new_basis, rayleigh)


def solution(mesh):
    in_specs = (P("space", None, None), P("vec", "space", None, None))
    out_specs = (P("vec", "space", None, None), P())
    return jax.shard_map(local, mesh=mesh, in_specs=in_specs, out_specs=out_specs, check_vma=False)
```

profile of v0, /device:TPU:0, one launch (start us, length us, event | category | flops | bytes accessed | tf_op | source)
XLA Modules:
  0.0 1709.0 jit_solution(7013803013438455873)
XLA Ops:
  7.2 2.6 copy.4
  9.9 38.5 %all-gather.3.cloned.1.call-done = f32[16,1,128,256]{2,0,3,1:T(8,128)} async-done(((f32[8,1,128,256]{2,0,3,1:T(8,128)}), f32[16,1,128,256]{2,0,3,1:T(8,128)}) %all-gather.3.cloned.1.call-update) | async-done | bytes 2097168 | tf_op jit(solution)/shard_map/all_gather | solution.py:53
  48.4 5.2 fusion.26
  53.6 171.0 %psum.70 = f32[16,16]{0,1:T(8,128)S(1)} all-reduce(f32[16,16]{0,1:T(8,128)S(1)} %fusion.26), channel_id=1, replica_groups=mesh['space'=64,'vec'=2] {'space'}, use_global_device_ids=true, to_apply=%region_0.0 | all-reduce | flops 256 | bytes 2048 | tf_op jit(solution)/shard_map/psum | solution.py:54
  224.7 1.5 cholesky.44
  226.2 0.6 compare_reduce_fusion.1
  226.8 0.6 fusion.68
  227.5 1.2 custom-call.6
  228.9 2.1 copy.7
  231.0 3.4 fusion.107
  234.5 2.6 fusion.36
  237.1 162.5 %psum.72 = f32[16,8]{0,1:T(8,128)S(1)} all-reduce(f32[16,8]{0,1:T(8,128)S(1)} %fusion.36), channel_id=1, replica_groups=mesh['space'=64,'vec'=2] {'space'}, use_global_device_ids=true, to_apply=%region_4.7 | all-reduce | flops 128 | bytes 1024 | tf_op jit(solution)/shard_map/psum | solution.py:66
  399.6 1.1 convolution_subtract_fusion
  401.1 0.5 collective-permute-start.3
  402.1 7.1 collective-permute-start
  409.2 0.4 collective-permute-start.1
  409.6 0.3 fusion.99
  410.4 3.1 collective-permute-done.2
  413.4 7.7 collective-permute-done.3
  421.1 0.8 fusion.46
  421.9 2.7 fusion.35
  424.7 7.7 collective-permute-done.1
  432.4 0.8 fusion.41
  433.2 2.6 fusion.37
  435.8 164.5 %all-reduce = (f32[16,8]{0,1:T(8,128)S(1)}, f32[16,8]{0,1:T(8,128)S(1)}) all-reduce(f32[16,8]{0,1:T(8,128)S(1)} %fusion.37, f32[16,8]{0,1:T(8,128)S(1)} %fusion.35), channel_id=1, replica_groups=mesh['space'=64,'vec'=2] {'space'}, use_global_device_ids=true, to_apply=%region_3.6 | all-reduce | flops 256 | bytes 2048 | tf_op jit(solution)/shard_map/psum | solution.py:60
  600.3 4.4 all_gather.10
  604.7 1.2 fusion.17
  605.9 1.3 fusion.18
  607.3 2.6 fusion.34
  609.9 162.5 %psum.74 = f32[16,8]{0,1:T(8,128)S(1)} all-reduce(f32[16,8]{0,1:T(8,128)S(1)} %fusion.34), channel_id=1, replica_groups=mesh['space'=64,'vec'=2] {'space'}, use_global_device_ids=true, to_apply=%region_6.9 | all-reduce | flops 128 | bytes 1024 | tf_op jit(solution)/shard_map/psum | solution.py:66
  772.4 1.1 fusion.13
  773.6 0.6 collective-permute-start.5
  775.0 11.0 collective-permute-done.4
  785.9 7.9 collective-permute-done.5
  793.8 0.8 fusion.51
  794.6 1.0 copy-done.5
  795.6 2.7 fusion.33
  798.3 162.5 %psum.75 = f32[16,8]{0,1:T(8,128)S(1)} all-reduce(f32[16,8]{0,1:T(8,128)S(1)} %fusion.33), channel_id=1, replica_groups=mesh['space'=64,'vec'=2] {'space'}, use_global_device_ids=true, to_apply=%region_7.10 | all-reduce | flops 128 | bytes 1024 | tf_op jit(solution)/shard_map/psum | solution.py:70
  960.8 3.1 fusion.20
  963.9 2.6 fusion.32
  966.5 162.5 %psum.76 = f32[16,8]{0,1:T(8,128)S(1)} all-reduce(f32[16,8]{0,1:T(8,128)S(1)} %fusion.32), channel_id=1, replica_groups=mesh['space'=64,'vec'=2] {'space'}, use_global_device_ids=true, to_apply=%region_8.11 | all-reduce | flops 128 | bytes 1024 | tf_op jit(solution)/shard_map/psum | solution.py:66
  1129.0 1.1 fusion.10
  1130.2 0.5 collective-permute-start.7
  1131.4 11.1 collective-permute-done.6
  1142.5 7.7 collective-permute-done.7
  1150.3 0.8 fusion.56
  1151.0 1.0 copy-done.4
  1152.0 2.7 fusion.31
  1154.7 162.7 %psum.77 = f32[16,8]{0,1:T(8,128)S(1)} all-reduce(f32[16,8]{0,1:T(8,128)S(1)} %fusion.31), channel_id=1, replica_groups=mesh['space'=64,'vec'=2] {'space'}, use_global_device_ids=true, to_apply=%region_9.12 | all-reduce | flops 128 | bytes 1024 | tf_op jit(solution)/shard_map/psum | solution.py:70
  1317.4 2.9 fusion.22
  1320.3 1.0 copy-done.6
  1321.2 2.7 fusion.30
  1323.9 162.5 %psum.78 = f32[16,8]{0,1:T(8,128)S(1)} all-reduce(f32[16,8]{0,1:T(8,128)S(1)} %fusion.30), channel_id=1, replica_groups=mesh['space'=64,'vec'=2] {'space'}, use_global_device_ids=true, to_apply=%region_10.13 | all-reduce | flops 128 | bytes 1024 | tf_op jit(solution)/shard_map/psum | solution.py:73
  1486.4 3.3 fusion.7
  1489.7 0.7 copy.15
  1490.4 28.6 %all-gather.5.cloned.1.call-done = f32[16,1,128,256]{3,0,2,1:T(8,128)} async-done(((f32[8,1,128,256]{3,0,2,1:T(8,128)}), f32[16,1,128,256]{3,0,2,1:T(8,128)}) %all-gather.5.cloned.1.call-update) | async-done | bytes 2097168 | tf_op jit(solution)/shard_map/all_gather | solution.py:75
  1518.9 5.2 fusion.27
  1524.2 171.0 %psum.79 = f32[16,16]{0,1:T(8,128)S(1)} all-reduce(f32[16,16]{0,1:T(8,128)S(1)} %fusion.27), channel_id=1, replica_groups=mesh['space'=64,'vec'=2] {'space'}, use_global_device_ids=true, to_apply=%region_11.14 | all-reduce | flops 256 | bytes 2048 | tf_op jit(solution)/shard_map/psum | solution.py:76
  1695.2 1.5 cholesky.55
  1696.7 0.6 compare_reduce_fusion
  1697.4 0.6 fusion.69
  1698.0 1.2 custom-call.7
  1699.5 1.1 fusion.4
  1700.6 1.3 copy.14
  (50 shorter events, 3.7 us)
Async XLA Ops:
  7.2 2.7 copy-start.9
  7.2 41.2 %all-gather.3.cloned.1.call-start = ((), (), s32[]{:S(2)}) async-start(), calls=%async_computation | async-start | bytes 3145728 | tf_op jit(solution)/shard_map/all_gather | solution.py:53
  9.8 1509.1 %all-gather.5.cloned.1.call-start = ((), (), s32[]{:S(2)}) async-start(), calls=%async_computation.1 | async-start | bytes 3145728 | tf_op jit(solution)/shard_map/all_gather | solution.py:75
  48.4 180.5 %copy-start.7 = (f32[16,1,128,256]{2,0,3,1:T(8,128)S(1)}, f32[16,1,128,256]{2,0,3,1:T(8,128)}, u32[]{:S(2)}) copy-start(f32[16,1,128,256]{2,0,3,1:T(8,128)} %all-gather.3.cloned.1.call-done) | copy-start | bytes 6291460
  401.0 12.4 collective-permute-start.2
  401.1 20.0 %collective-permute-start.3 = (f32[8,1,128,256]{3,0,2,1:T(8,128)S(1)}, f32[8,1,128,256]{3,0,2,1:T(8,128)S(1)}, u32[]{:S(2)}, u32[]{:S(2)}) collective-permute-start(f32[8,1,128,256]{3,0,2,1:T(8,128)S(1)} %bitcast.203), channel_id=1, source_target_pairs={{0,2},{2,4},{4,6},{6,8},{8,10},{10,12},{12,14},{14,16},{16,18},{18... | collective-permute-start | bytes 3145736 | tf_op jit(solution)/shard_map/ppermute | solution.py:18
  402.1 22.6 %collective-permute-start = (f32[8,1,128,256]{3,0,2,1:T(8,128)S(1)}, f32[8,1,128,256]{3,0,2,1:T(8,128)S(1)}, u32[]{:S(2)}, u32[]{:S(2)}) collective-permute-start(f32[8,1,128,256]{3,0,2,1:T(8,128)S(1)} %dynamic-slice_bitcast_fusion), channel_id=1, source_target_pairs={{2,0},{4,2},{6,4},{8,6},{10,8},{12,10},{14,12},{16,14},{18,16},{20... | collective-permute-start | bytes 3145736 | tf_op jit(solution)/shard_map/ppermute | solution.py:19
  409.2 23.2 %collective-permute-start.1 = (f32[8,1,128,256]{3,0,2,1:T(8,128)S(1)}, f32[8,1,128,256]{3,0,2,1:T(8,128)S(1)}, u32[]{:S(2)}, u32[]{:S(2)}) collective-permute-start(f32[8,1,128,256]{3,0,2,1:T(8,128)S(1)} %dynamic-slice_bitcast_fusion), channel_id=1, source_target_pairs={{0,2},{2,4},{4,6},{6,8},{8,10},{10,12},{12,14},{14,16},{16,18},{18... | collective-permute-start | bytes 3145736 | tf_op jit(solution)/shard_map/ppermute | solution.py:18
  421.9 11.3 copy-start.2
  604.7 1.2 copy-start.3
  605.9 1.4 copy-start.1
  607.2 166.3 %copy-start = (f32[8,1,128,256]{3,0,2,1:T(8,128)}, f32[8,1,128,256]{3,0,2,1:T(8,128)S(1)}, u32[]{:S(2)}) copy-start(f32[8,1,128,256]{3,0,2,1:T(8,128)S(1)} %fusion.18) | copy-start | bytes 3145732
  773.5 12.4 collective-permute-start.4
  773.6 20.2 %collective-permute-start.5 = (f32[8,1,128,256]{3,0,2,1:T(8,128)S(1)}, f32[8,1,128,256]{3,0,2,1:T(8,128)S(1)}, u32[]{:S(2)}, u32[]{:S(2)}) collective-permute-start(f32[8,1,128,256]{3,0,2,1:T(8,128)S(1)} %fusion.13), channel_id=1, source_target_pairs={{0,2},{2,4},{4,6},{6,8},{8,10},{10,12},{12,14},{14,16},{16,18},{18... | collective-permute-start | bytes 3145736 | tf_op jit(solution)/shard_map/ppermute | solution.py:18
  794.6 1.0 copy-start.5
  1130.2 12.4 collective-permute-start.6
  1130.2 20.0 %collective-permute-start.7 = (f32[8,1,128,256]{3,0,2,1:T(8,128)S(1)}, f32[8,1,128,256]{3,0,2,1:T(8,128)S(1)}, u32[]{:S(2)}, u32[]{:S(2)}) collective-permute-start(f32[8,1,128,256]{3,0,2,1:T(8,128)S(1)} %fusion.10), channel_id=1, source_target_pairs={{0,2},{2,4},{4,6},{6,8},{8,10},{10,12},{12,14},{14,16},{16,18},{18... | collective-permute-start | bytes 3145736 | tf_op jit(solution)/shard_map/ppermute | solution.py:18
  1151.0 1.0 copy-start.4
  1320.2 1.0 copy-start.6
  1518.9 180.5 %copy-start.8 = (f32[16,1,128,256]{3,0,2,1:T(8,128)S(1)}, f32[16,1,128,256]{3,0,2,1:T(8,128)}, u32[]{:S(2)}) copy-start(f32[16,1,128,256]{3,0,2,1:T(8,128)} %all-gather.5.cloned.1.call-done) | copy-start | bytes 6291460
Sparse Core Ops, SparseCore 0:
  10.2 38.1 all-gather.2
  1489.8 29.0 all-gather.4
where the time goes:
time: 1720 us; the launch traced here: 1710 us
  blocking collectives  1490 us (87%)
  waiting for transfers between devices  123 us (7%)
  matrix products  51.6 us (3%)
    psum x3, blocking collectives, local(): coeff = lax.psum(local_inner(basis_all, correction, scale), 'space')  488 us
    psum x2, blocking collectives, local(): back = lax.psum(local_inner(basis_all, moved, scale), 'space')  325 us
    psum x1, blocking collectives, local(): gram_two = lax.psum(local_inner(fresh_all, fresh_all, scale), 'space')  171 us
    psum x1, blocking collectives, local(): gram = lax.psum(local_inner(whole, whole, scale), 'space')  171 us
    psum x1, blocking collectives, local(): panel = lax.psum(local_inner(basis_all, image, scale), 'space')  165 us
    psum x1, blocking collectives, local(): proj_two = lax.psum(local_inner(basis_all, correction, scale), 'space')  163 us
    all_gather x1, waiting for transfers between devices, local(): whole = lax.all_gather(start_basis, 'vec', axis=0, tiled=True)  38.5 us
  transfers between devices with their start and end apart: 10, of which 10 were waited for; matrix products, arithmetic and copies ran while one was open for 0% of the time, Pallas kernels for 0%

commit v1 on v0

--- a/solution.py
+++ b/solution.py
@@ -45,6 +45,10 @@
 
 
 def local(potential, start_basis):
+
+    def _post_entries(my_data, axis_key):
+        return jnp.sum(lax.all_gather(my_data, axis_key), axis=0)
+
     mine = start_basis.shape[0]
     scale = 1.0 / (
         start_basis.shape[1] * start_basis.shape[2] * start_basis.shape[3] * lax.axis_size("space")
@@ -70,7 +74,7 @@
         back = lax.psum(local_inner(basis_all, moved, scale), "space")
         update = -resid - (moved - combine(back, basis_all))
         correction = correction + update / shifted
-    proj_two = lax.psum(local_inner(basis_all, correction, scale), "space")
+    proj_two = _post_entries(local_inner(basis_all, correction, scale), "space")
     fresh = correction - combine(proj_two, basis_all)
     fresh_all = lax.all_gather(fresh, "vec", axis=0, tiled=True)
     gram_two = lax.psum(local_inner(fresh_all, fresh_all, scale), "space")

time: 1720 us -> 1650 us (0.959)
  blocking collectives: 1490 us -> 1410 us
    psum x1 -> x0, blocking collectives: 163 us -> none  [local(): proj_two = lax.psum(local_inner(basis_all, correction, scale), 'space')]
    all_gather x0 -> x1, blocking collectives: none -> 88.9 us  [_post_entries(): return jnp.sum(lax.all_gather(my_data, axis_key), axis=0)]
where the time goes in v1:
time: 1650 us; the launch traced here: 1640 us
  blocking collectives  1410 us (85%)
  waiting for transfers between devices  125 us (8%)
  matrix products  51.6 us (3%)
    psum x3, blocking collectives, local(): coeff = lax.psum(local_inner(basis_all, correction, scale), 'space')  488 us
    psum x2, blocking collectives, local(): back = lax.psum(local_inner(basis_all, moved, scale), 'space')  325 us
    psum x1, blocking collectives, local(): gram_two = lax.psum(local_inner(fresh_all, fresh_all, scale), 'space')  171 us
    psum x1, blocking collectives, local(): gram = lax.psum(local_inner(whole, whole, scale), 'space')  171 us
    psum x1, blocking collectives, local(): panel = lax.psum(local_inner(basis_all, image, scale), 'space')  165 us
    all_gather x1, blocking collectives, _post_entries(): return jnp.sum(lax.all_gather(my_data, axis_key), axis=0)  88.9 us
    all_gather x1, waiting for transfers between devices, local(): whole = lax.all_gather(start_basis, 'vec', axis=0, tiled=True)  38.5 us
  transfers between devices with their start and end apart: 10, of which 10 were waited for; matrix products, arithmetic and copies ran while one was open for 0% of the time, Pallas kernels for 0%

profile of v1, /device:TPU:0, one launch (start us, length us, event | category | flops | bytes accessed | tf_op | source)
XLA Modules:
  0.0 1637.2 jit_solution(853357354743582278)
XLA Ops:
  7.2 2.6 copy.18
  9.9 38.5 %all-gather.5.cloned.1.call-done = f32[16,1,128,256]{2,0,3,1:T(8,128)} async-done(((f32[8,1,128,256]{2,0,3,1:T(8,128)}), f32[16,1,128,256]{2,0,3,1:T(8,128)}) %all-gather.5.cloned.1.call-update) | async-done | bytes 2097168 | tf_op jit(solution)/shard_map/all_gather | solution.py:57
  48.4 5.2 fusion.26
  53.6 171.0 %psum.63 = f32[16,16]{0,1:T(8,128)S(1)} all-reduce(f32[16,16]{0,1:T(8,128)S(1)} %fusion.26), channel_id=1, replica_groups=mesh['space'=64,'vec'=2] {'space'}, use_global_device_ids=true, to_apply=%region_0.0 | all-reduce | flops 256 | bytes 2048 | tf_op jit(solution)/shard_map/psum | solution.py:58
  224.7 1.5 cholesky.44
  226.2 0.6 compare_reduce_fusion.1
  226.8 0.6 fusion.69
  227.5 1.2 custom-call.6
  228.9 2.1 copy.21
  231.0 3.4 fusion.108
  234.5 2.6 fusion.37
  237.1 162.5 %psum.65 = f32[16,8]{0,1:T(8,128)S(1)} all-reduce(f32[16,8]{0,1:T(8,128)S(1)} %fusion.37), channel_id=1, replica_groups=mesh['space'=64,'vec'=2] {'space'}, use_global_device_ids=true, to_apply=%region_4.7 | all-reduce | flops 128 | bytes 1024 | tf_op jit(solution)/shard_map/psum | solution.py:70
  399.6 1.1 convolution_subtract_fusion
  401.1 0.5 collective-permute-start.3
  402.1 7.1 collective-permute-start
  409.2 0.4 collective-permute-start.1
  409.6 0.3 fusion.100
  410.4 3.1 collective-permute-done.2
  413.4 7.7 collective-permute-done.3
  421.1 0.8 fusion.47
  421.9 2.7 fusion.36
  424.7 7.7 collective-permute-done.1
  432.4 0.8 fusion.42
  433.2 2.6 fusion.38
  435.8 164.5 %all-reduce = (f32[16,8]{0,1:T(8,128)S(1)}, f32[16,8]{0,1:T(8,128)S(1)}) all-reduce(f32[16,8]{0,1:T(8,128)S(1)} %fusion.38, f32[16,8]{0,1:T(8,128)S(1)} %fusion.36), channel_id=1, replica_groups=mesh['space'=64,'vec'=2] {'space'}, use_global_device_ids=true, to_apply=%region_3.6 | all-reduce | flops 256 | bytes 2048 | tf_op jit(solution)/shard_map/psum | solution.py:64
  600.3 4.4 all_gather.16
  604.7 1.2 fusion.17
  605.9 1.3 fusion.18
  607.3 2.6 fusion.35
  609.9 162.5 %psum.67 = f32[16,8]{0,1:T(8,128)S(1)} all-reduce(f32[16,8]{0,1:T(8,128)S(1)} %fusion.35), channel_id=1, replica_groups=mesh['space'=64,'vec'=2] {'space'}, use_global_device_ids=true, to_apply=%region_6.9 | all-reduce | flops 128 | bytes 1024 | tf_op jit(solution)/shard_map/psum | solution.py:70
  772.4 1.1 fusion.13
  773.6 0.6 collective-permute-start.5
  775.0 11.0 collective-permute-done.4
  785.9 7.9 collective-permute-done.5
  793.8 0.8 fusion.52
  794.6 1.0 copy-done.5
  795.6 2.7 fusion.34
  798.3 162.5 %psum.68 = f32[16,8]{0,1:T(8,128)S(1)} all-reduce(f32[16,8]{0,1:T(8,128)S(1)} %fusion.34), channel_id=1, replica_groups=mesh['space'=64,'vec'=2] {'space'}, use_global_device_ids=true, to_apply=%region_7.10 | all-reduce | flops 128 | bytes 1024 | tf_op jit(solution)/shard_map/psum | solution.py:74
  960.8 3.1 fusion.20
  963.9 2.6 fusion.33
  966.5 162.5 %psum.69 = f32[16,8]{0,1:T(8,128)S(1)} all-reduce(f32[16,8]{0,1:T(8,128)S(1)} %fusion.33), channel_id=1, replica_groups=mesh['space'=64,'vec'=2] {'space'}, use_global_device_ids=true, to_apply=%region_8.11 | all-reduce | flops 128 | bytes 1024 | tf_op jit(solution)/shard_map/psum | solution.py:70
  1129.0 1.1 fusion.10
  1130.2 0.5 collective-permute-start.7
  1131.4 11.1 collective-permute-done.6
  1142.5 7.7 collective-permute-done.7
  1150.3 0.8 fusion.57
  1151.0 1.0 copy-done.4
  1152.0 2.7 fusion.32
  1154.7 162.7 %psum.70 = f32[16,8]{0,1:T(8,128)S(1)} all-reduce(f32[16,8]{0,1:T(8,128)S(1)} %fusion.32), channel_id=1, replica_groups=mesh['space'=64,'vec'=2] {'space'}, use_global_device_ids=true, to_apply=%region_9.12 | all-reduce | flops 128 | bytes 1024 | tf_op jit(solution)/shard_map/psum | solution.py:74
  1317.4 2.9 fusion.22
  1320.3 1.0 copy-done.6
  1321.2 2.7 fusion.31
  1323.9 88.9 %all-gather.1 = f32[64,16,8]{1,2,0:T(8,128)S(1)} all-gather(f32[1,16,8]{1,2,0:T(8,128)S(1)} %fusion.31), channel_id=2, replica_groups=mesh['space'=64,'vec'=2] {'space'}, dimensions={0}, use_global_device_ids=true | all-gather | bytes 33280 | tf_op jit(solution)/shard_map/all_gather | solution.py:50
  1412.8 3.3 fusion.7
  1416.1 0.7 copy.31
  1416.8 30.4 %all-gather.7.cloned.1.call-done = f32[16,1,128,256]{3,0,2,1:T(8,128)} async-done(((f32[8,1,128,256]{3,0,2,1:T(8,128)}), f32[16,1,128,256]{3,0,2,1:T(8,128)}) %all-gather.7.cloned.1.call-update) | async-done | bytes 2097168 | tf_op jit(solution)/shard_map/all_gather | solution.py:79
  1447.2 5.2 fusion.27
  1452.4 171.0 %psum.71 = f32[16,16]{0,1:T(8,128)S(1)} all-reduce(f32[16,16]{0,1:T(8,128)S(1)} %fusion.27), channel_id=1, replica_groups=mesh['space'=64,'vec'=2] {'space'}, use_global_device_ids=true, to_apply=%region_11.14 | all-reduce | flops 256 | bytes 2048 | tf_op jit(solution)/shard_map/psum | solution.py:80
  1623.5 1.5 cholesky.55
  1625.0 0.6 compare_reduce_fusion
  1625.6 0.6 fusion.70
  1626.3 1.2 custom-call.7
  1627.7 1.1 fusion.4
  1628.9 1.3 copy.30
  (51 shorter events, 3.7 us)
Async XLA Ops:
  7.2 2.7 copy-start.9
  7.2 41.2 %all-gather.5.cloned.1.call-start = ((), (), s32[]{:S(2)}) async-start(), calls=%async_computation | async-start | bytes 3145728 | tf_op jit(solution)/shard_map/all_gather | solution.py:57
  9.8 1437.4 %all-gather.7.cloned.1.call-start = ((), (), s32[]{:S(2)}) async-start(), calls=%async_computation.1 | async-start | bytes 3145728 | tf_op jit(solution)/shard_map/all_gather | solution.py:79
  48.4 180.5 %copy-start.7 = (f32[16,1,128,256]{2,0,3,1:T(8,128)S(1)}, f32[16,1,128,256]{2,0,3,1:T(8,128)}, u32[]{:S(2)}) copy-start(f32[16,1,128,256]{2,0,3,1:T(8,128)} %all-gather.5.cloned.1.call-done) | copy-start | bytes 6291460
  401.0 12.4 collective-permute-start.2
  401.1 20.0 %collective-permute-start.3 = (f32[8,1,128,256]{3,0,2,1:T(8,128)S(1)}, f32[8,1,128,256]{3,0,2,1:T(8,128)S(1)}, u32[]{:S(2)}, u32[]{:S(2)}) collective-permute-start(f32[8,1,128,256]{3,0,2,1:T(8,128)S(1)} %bitcast.207), channel_id=1, source_target_pairs={{0,2},{2,4},{4,6},{6,8},{8,10},{10,12},{12,14},{14,16},{16,18},{18... | collective-permute-start | bytes 3145736 | tf_op jit(solution)/shard_map/ppermute | solution.py:18
  402.1 22.6 %collective-permute-start = (f32[8,1,128,256]{3,0,2,1:T(8,128)S(1)}, f32[8,1,128,256]{3,0,2,1:T(8,128)S(1)}, u32[]{:S(2)}, u32[]{:S(2)}) collective-permute-start(f32[8,1,128,256]{3,0,2,1:T(8,128)S(1)} %dynamic-slice_bitcast_fusion), channel_id=1, source_target_pairs={{2,0},{4,2},{6,4},{8,6},{10,8},{12,10},{14,12},{16,14},{18,16},{20... | collective-permute-start | bytes 3145736 | tf_op jit(solution)/shard_map/ppermute | solution.py:19
  409.2 23.2 %collective-permute-start.1 = (f32[8,1,128,256]{3,0,2,1:T(8,128)S(1)}, f32[8,1,128,256]{3,0,2,1:T(8,128)S(1)}, u32[]{:S(2)}, u32[]{:S(2)}) collective-permute-start(f32[8,1,128,256]{3,0,2,1:T(8,128)S(1)} %dynamic-slice_bitcast_fusion), channel_id=1, source_target_pairs={{0,2},{2,4},{4,6},{6,8},{8,10},{10,12},{12,14},{14,16},{16,18},{18... | collective-permute-start | bytes 3145736 | tf_op jit(solution)/shard_map/ppermute | solution.py:18
  421.9 11.3 copy-start.2
  604.7 1.2 copy-start.3
  605.9 1.4 copy-start.1
  607.2 166.3 %copy-start = (f32[8,1,128,256]{3,0,2,1:T(8,128)}, f32[8,1,128,256]{3,0,2,1:T(8,128)S(1)}, u32[]{:S(2)}) copy-start(f32[8,1,128,256]{3,0,2,1:T(8,128)S(1)} %fusion.18) | copy-start | bytes 3145732
  773.5 12.4 collective-permute-start.4
  773.6 20.2 %collective-permute-start.5 = (f32[8,1,128,256]{3,0,2,1:T(8,128)S(1)}, f32[8,1,128,256]{3,0,2,1:T(8,128)S(1)}, u32[]{:S(2)}, u32[]{:S(2)}) collective-permute-start(f32[8,1,128,256]{3,0,2,1:T(8,128)S(1)} %fusion.13), channel_id=1, source_target_pairs={{0,2},{2,4},{4,6},{6,8},{8,10},{10,12},{12,14},{14,16},{16,18},{18... | collective-permute-start | bytes 3145736 | tf_op jit(solution)/shard_map/ppermute | solution.py:18
  794.6 1.0 copy-start.5
  1130.2 12.4 collective-permute-start.6
  1130.2 20.0 %collective-permute-start.7 = (f32[8,1,128,256]{3,0,2,1:T(8,128)S(1)}, f32[8,1,128,256]{3,0,2,1:T(8,128)S(1)}, u32[]{:S(2)}, u32[]{:S(2)}) collective-permute-start(f32[8,1,128,256]{3,0,2,1:T(8,128)S(1)} %fusion.10), channel_id=1, source_target_pairs={{0,2},{2,4},{4,6},{6,8},{8,10},{10,12},{12,14},{14,16},{16,18},{18... | collective-permute-start | bytes 3145736 | tf_op jit(solution)/shard_map/ppermute | solution.py:18
  1151.0 1.0 copy-start.4
  1320.2 1.0 copy-start.6
  1447.2 180.5 %copy-start.8 = (f32[16,1,128,256]{3,0,2,1:T(8,128)S(1)}, f32[16,1,128,256]{3,0,2,1:T(8,128)}, u32[]{:S(2)}) copy-start(f32[16,1,128,256]{3,0,2,1:T(8,128)} %all-gather.7.cloned.1.call-done) | copy-start | bytes 6291460
Sparse Core Ops, SparseCore 0:
  10.2 38.1 all-gather.4
  1416.3 30.9 all-gather.6
